TPU v7x, 128 devices: a whole 4x4x4 slice. The times are simulated.
128 devices in a mesh: rep: 64 (over z, y, x_hi, core), shard: 2 (over x_lo).
Axes of the slice: x: 4 (x_hi: 2, x_lo: 2; x = x_hi * 2 + x_lo), y: 4, z: 4, core: 2. Of those that a mesh axis runs over, the one named last changes fastest.
Arguments:
- grad_xproj: bfloat16 [256, 2, 3072, 128], P(('rep', 'shard')), may hold values from -32 to 32
- grad_chan: bfloat16 [256, 2, 118, 3072], P(('rep', 'shard')), may hold values from -32 to 32
- grad_embed: bfloat16 [256, 1024, 1536], P(('rep', 'shard')), may hold values from -32 to 32
- weight_xproj: float32 [2, 3072, 128], P(None, 'shard'), may hold values from -0.3125 to 0.3125
- weight_chan: float32 [2, 118, 3072], P(None, None, 'shard'), may hold values from -0.3125 to 0.3125
- weight_embed: float32 [1024, 1536], P('shard'), may hold values from -0.3125 to 0.3125
- moment_xproj: float32 [2, 3072, 128], P(None, 'shard'), may hold values from -0.015625 to 0.015625
- moment_chan: float32 [2, 118, 3072], P(None, None, 'shard'), may hold values from -0.015625 to 0.015625
- moment_embed: float32 [1024, 1536], P('shard'), may hold values from -0.015625 to 0.015625
- second_xproj: float32 [2, 3072, 128], P(None, 'shard'), may hold values from 1e-08 to 1e-05
- second_chan: float32 [2, 118, 3072], P(None, None, 'shard'), may hold values from 1e-08 to 1e-05
- second_embed: float32 [1024, 1536], P('shard'), may hold values from 1e-08 to 1e-05
Outputs:
- new_weight_xproj: float32 [2, 3072, 128], P(None, 'shard')
- new_weight_chan: float32 [2, 118, 3072], P(None, None, 'shard')
- new_weight_embed: float32 [1024, 1536], P('shard')
- new_moment_xproj: float32 [2, 3072, 128], P(None, 'shard')
- new_moment_chan: float32 [2, 118, 3072], P(None, None, 'shard')
- new_moment_embed: float32 [1024, 1536], P('shard')
- new_second_xproj: float32 [2, 3072, 128], P(None, 'shard')
- new_second_chan: float32 [2, 118, 3072], P(None, None, 'shard')
- new_second_embed: float32 [1024, 1536], P('shard')
- full_xproj: bfloat16 [2, 3072, 128], replicated
- full_chan: bfloat16 [2, 118, 3072], replicated
- full_embed: bfloat16 [1024, 1536], replicated
- pre_norm: float32 [1], replicated
All inputs are finite; a program needn't handle non-finite values.
Results may differ from a plain program's by a relative error of at most 0.00085.
Values may be sent and summed in bfloat16 or wider, within the bound.
No kernel may reach another device: no remote copies, remote signals or barrier semaphores. Data moves between devices by JAX's collectives and lax.ppermute only.
A program may use at most 448 MiB of HBM per device.

v0:
```python
import jax
import jax.numpy as jnp
from jax import lax
from jax.sharding import PartitionSpec as P

beta_one = 0.9
beta_two = 0.999
learn_rate = 0.003
decay_rate = 0.1
epsilon = 1e-08
correct_one = 0.9999734386011124
correct_two = 0.09520785288629094


def adamw_update(weight, moment, second, gradient, clip_factor):
    clipped = clip_factor * gradient
    new_moment = beta_one * moment + (1.0 - beta_one) * clipped
    new_second = beta_two * second + (1.0 - beta_two) * clipped * clipped
    step_size = new_moment / correct_one / (jnp.sqrt(new_second / correct_two) + epsilon)
    new_weight = weight - learn_rate * (step_size + decay_rate * weight)
    return (new_weight, new_moment, new_second)


def on_device(
    grad_xproj,
    grad_chan,
    grad_embed,
    weight_xproj,
    weight_chan,
    weight_embed,
    moment_xproj,
    moment_chan,
    moment_embed,
    second_xproj,
    second_chan,
    second_embed,
):
    count_rep = lax.axis_size("rep")
    count_shard = lax.axis_size("shard")
    summed_x = jnp.sum(grad_xproj, axis=0, dtype=jnp.float32)
    summed_c = jnp.sum(grad_chan, axis=0, dtype=jnp.float32)
    summed_e = jnp.sum(grad_embed, axis=0, dtype=jnp.float32)
    group = (
        lax.psum_scatter(
            summed_x.astype(jnp.bfloat16), "shard", scatter_dimension=1, tiled=True
        ).astype(jnp.float32),
        lax.psum_scatter(
            summed_c.astype(jnp.bfloat16), "shard", scatter_dimension=2, tiled=True
        ).astype(jnp.float32),
        lax.psum_scatter(
            summed_e.astype(jnp.bfloat16), "shard", scatter_dimension=0, tiled=True
        ).astype(jnp.float32),
    )
    blocks = lax.psum((group[0], group[1], group[2]), "rep")
    inverse = 1.0 / (grad_xproj.shape[0] * count_rep * count_shard)
    mean_x = blocks[0] * inverse
    mean_c = blocks[1] * inverse
    mean_e = blocks[2] * inverse
    partial_squares = jnp.sum(mean_x * mean_x) + jnp.sum(mean_c * mean_c) + jnp.sum(mean_e * mean_e)
    squares = lax.psum(partial_squares, "shard")
    norm_value = jnp.sqrt(squares)
    clip_factor = jnp.minimum(1.0, 1.0 / (norm_value + 1e-06))
    wx, mx, vx = adamw_update(weight_xproj, moment_xproj, second_xproj, mean_x, clip_factor)
    wc, mc, vc = adamw_update(weight_chan, moment_chan, second_chan, mean_c, clip_factor)
    we, me, ve = adamw_update(weight_embed, moment_embed, second_embed, mean_e, clip_factor)
    gathered = (
        lax.all_gather(wx.astype(jnp.bfloat16), "shard", axis=1, tiled=True),
        lax.all_gather(wc.astype(jnp.bfloat16), "shard", axis=2, tiled=True),
        lax.all_gather(we.astype(jnp.bfloat16), "shard", axis=0, tiled=True),
    )
    return (
        wx,
        wc,
        we,
        mx,
        mc,
        me,
        vx,
        vc,
        ve,
        gathered[0],
        gathered[1],
        gathered[2],
        jnp.reshape(norm_value, (1,)),
    )


def solution(mesh):
    placed = (
        P(("rep", "shard"), None, None, None),
        P(("rep", "shard"), None, None, None),
        P(("rep", "shard"), None, None),
        P(None, "shard", None),
        P(None, None, "shard"),
        P("shard", None),
        P(None, "shard", None),
        P(None, None, "shard"),
        P("shard", None),
        P(None, "shard", None),
        P(None, None, "shard"),
        P("shard", None),
    )
    return jax.shard_map(
        on_device,
        mesh=mesh,
        in_specs=placed,
        out_specs=(
            P(None, "shard", None),
            P(None, None, "shard"),
            P("shard", None),
            P(None, "shard", None),
            P(None, None, "shard"),
            P("shard", None),
            P(None, "shard", None),
            P(None, None, "shard"),
            P("shard", None),
            P(),
            P(),
            P(),
            P(),
        ),
        check_vma=False,
    )
```

profile of v0, /device:TPU:1, one launch (start us, length us, event | category | flops | bytes accessed | tf_op | source)
XLA Modules:
  0.0 806.5 jit_solution(3559955693259106270)
XLA Ops:
  7.2 0.0 reduce-scatter.10.cloned.1.call-start
  7.2 6.5 reduce_sum.65
  13.7 66.3 %copy.25 = bf16[2,118,3072]{0,1,2:T(8,128)(2,1)} copy(bf16[2,118,3072]{2,0,1:T(2,128)(2,1)S(1)} %reduce_sum.65) | data formatting | bytes 2899968
  80.0 86.8 %reshape.30 = bf16[3072,236]{1,0:T(8,128)(2,1)} reshape(bf16[3072,118,2]{2,1,0:T(8,128)(2,1)} %bitcast.1) | data formatting | bytes 2899968
  166.8 0.0 reduce-scatter.10.cloned.1.call-update
  166.8 0.0 reduce-scatter.6.cloned.1.call-start
  166.9 2.2 reduce_sum.63
  169.0 0.0 reduce-scatter.6.cloned.1.call-update
  169.1 0.0 reduce-scatter.8.cloned.1.call-start
  169.1 6.5 reduce_sum.67
  175.6 0.0 reduce-scatter.8.cloned.1.call-update
  175.6 0.2 all-gather.6.cloned.1.call-start
  175.9 22.9 %reduce-scatter.10.cloned.1.call-done = bf16[1536,236]{1,0:T(8,128)(2,1)} async-done(((bf16[3072,236]{1,0:T(8,128)(2,1)}), bf16[1536,236]{1,0:T(8,128)(2,1)}) %reduce-scatter.10.cloned.1.call-update) | async-done | bytes 725008
  198.8 37.8 %reshape.31 = bf16[1536,118,2]{2,1,0:T(8,128)(2,1)} reshape(bf16[1536,236]{1,0:T(8,128)(2,1)} %reduce-scatter.10.cloned.1.call-done) | data formatting | bytes 1449984
  236.6 41.9 %copy.26 = bf16[2,118,1536]{2,0,1:T(2,128)(2,1)} copy(bf16[2,118,1536]{0,1,2:T(8,128)(2,1)} %bitcast.4) | data formatting | bytes 1449984
  278.5 2.7 reduce-scatter.8.cloned.1.call-done
  281.2 373.8 %all-reduce.2 = (f32[2,1536,128]{2,1,0:T(8,128)}, f32[2,118,1536]{2,0,1:T(2,128)}, f32[512,1536]{1,0:T(8,128)S(1)}) all-reduce(bf16[2,1536,128]{2,1,0:T(8,128)(2,1)} %reduce-scatter.6.cloned.1.call-done, bf16[2,118,1536]{2,0,1:T(2,128)(2,1)} %copy.26, ...), channel_id=1, replica_groups=mesh['rep'=64,'shard'=2] {'rep'}, use_global_device_ids=true, to_apply=%region_2.0 | all-reduce | flops 1542144 | bytes 9252864 | tf_op jit(solution)/shard_map/psum | solution.py:54
  654.9 2.5 multiply_reduce_fusion.1
  657.5 2.1 multiply_reduce_fusion.2
  659.6 1.4 multiply_reduce_fusion
  662.9 4.3 psum.31
  667.9 8.4 %fusion.5 = (bf16[2,118,1536]{2,0,1:T(2,128)(2,1)}, f32[2,118,1536]{2,0,1:T(2,128)}, f32[2,118,1536]{2,0,1:T(2,128)}, f32[2,118,1536]{2,0,1:T(2,128)}) fusion(f32[2,118,1536]{2,0,1:T(2,128)} %param.16, f32[2,118,1536]{2,0,1:T(2,128)} %get-tuple-element.14, f32[]{:T(128)S(6)} %mul.157, f32[2,118,1536]{2,0,1:T(2,128)} %param.19, f32[2,118,1536]{2,0,1:T(2,128)} %param.22), kind=kLoop, calls=%fused_computation.16 | loop fusion | flops 6162432 | bytes 10874884 | tf_op jit(solution)/shard_map/convert_element_type | solution.py:68
  676.4 0.0 all-gather.4.cloned.1.call-start
  676.5 6.1 fusion.7
  682.6 0.3 all-gather.8.cloned.1.call-start
  682.8 7.4 fusion.3
  690.2 16.8 %all-gather.6.cloned.1.call-done = bf16[2,118,3072]{2,0,1:T(2,128)(2,1)} async-done(((bf16[2,118,1536]{2,0,1:T(2,128)(2,1)}), bf16[2,118,3072]{2,0,1:T(2,128)(2,1)}) %all-gather.6.cloned.1.call-update) | async-done | bytes 1450000 | tf_op jit(solution)/shard_map/all_gather | solution.py:68
  707.0 32.9 %all-gather.4.cloned.1.call-done = bf16[2,3072,128]{2,1,0:T(8,128)(2,1)} async-done(((bf16[2,1536,128]{2,1,0:T(8,128)(2,1)}), bf16[2,3072,128]{2,1,0:T(8,128)(2,1)}) %all-gather.4.cloned.1.call-update) | async-done | bytes 1572880 | tf_op jit(solution)/shard_map/all_gather | solution.py:67
  739.9 50.6 %all-gather.8.cloned.1.call-done = bf16[1024,1536]{1,0:T(8,128)(2,1)} async-done(((bf16[512,1536]{1,0:T(8,128)(2,1)}), bf16[1024,1536]{1,0:T(8,128)(2,1)}) %all-gather.8.cloned.1.call-update) | async-done | bytes 3145744 | tf_op jit(solution)/shard_map/all_gather | solution.py:69
  790.6 2.8 copy.36
  793.4 3.5 copy.37
  796.9 1.7 copy.38
  (10 shorter events, 0.1 us)
Async XLA Ops:
  7.2 191.6 %reduce-scatter.10.cloned.1.call-start = ((), (), s32[]{:S(2)}) async-start(), calls=%async_computation.8 | async-start | bytes 2359296
  80.0 86.8 %copy-start.1 = (bf16[2,2,3072,128]{3,2,1,0:T(8,128)(2,1)S(1)}, bf16[2,2,3072,128]{3,2,1,0:T(8,128)(2,1)}, u32[]{:S(2)}) copy-start(bf16[2,2,3072,128]{3,2,1,0:T(8,128)(2,1)} %param.12) | copy-start | bytes 9437188
  166.8 111.7 %reduce-scatter.6.cloned.1.call-start = ((), (), s32[]{:S(2)}) async-start(), calls=%async_computation.3 | async-start | bytes 2359296 | tf_op jit(solution)/shard_map/reduce_scatter | solution.py:44
  169.1 112.1 %reduce-scatter.8.cloned.1.call-start = ((), (), s32[]{:S(2)}) async-start(), calls=%async_computation.4 | async-start | bytes 4718592 | tf_op jit(solution)/shard_map/reduce_scatter | solution.py:50
  175.6 531.4 %all-gather.6.cloned.1.call-start = ((), (), s32[]{:S(2)}) async-start(), calls=%async_computation.6 | async-start | bytes 2174976 | tf_op jit(solution)/shard_map/all_gather | solution.py:68
  654.9 2.5 copy-start
  676.4 63.5 %all-gather.4.cloned.1.call-start = ((), (), s32[]{:S(2)}) async-start(), calls=%async_computation.5 | async-start | bytes 2359296 | tf_op jit(solution)/shard_map/all_gather | solution.py:67
  682.6 108.0 %all-gather.8.cloned.1.call-start = ((), (), s32[]{:S(2)}) async-start(), calls=%async_computation.7 | async-start | bytes 4718592 | tf_op jit(solution)/shard_map/all_gather | solution.py:69
  790.6 6.3 copy-start.2
Sparse Core Ops, SparseCore 0:
  166.9 31.7 reduce-scatter.9
  201.8 29.5 reduce-scatter.5
  234.3 46.8 reduce-scatter.7
  676.5 30.4 all-gather.5
  709.2 30.6 all-gather.3
  742.1 48.4 all-gather.7
where the time goes:
time: 810 us; the launch traced here: 806 us
  blocking collectives  378 us (47%)
  local copies, waits for them, and re-layouts  241 us (30%)
  waiting for transfers between devices  126 us (16%)
  other arithmetic  43.1 us (5%)
  between operations  18 us (2%)
    psum x1, blocking collectives, on_device(): blocks = lax.psum((group[0], group[1], group[2]), 'rep')  374 us
    unnamed x13, local copies, waits for them, and re-layouts  241 us
    all_gather x1, waiting for transfers between devices, on_device(): lax.all_gather(we.astype(jnp.bfloat16), 'shard', axis=0, tiled=True)  50.6 us
    all_gather x1, waiting for transfers between devices, on_device(): lax.all_gather(wx.astype(jnp.bfloat16), 'shard', axis=1, tiled=True)  32.9 us
    unnamed x7, waiting for transfers between devices  23 us
    all_gather x1, waiting for transfers between devices, on_device(): lax.all_gather(wc.astype(jnp.bfloat16), 'shard', axis=2, tiled=True)  16.8 us
  transfers between devices with their start and end apart: 6, of which 5 were waited for; matrix products, arithmetic and copies ran while one was open for 13% of the time, Pallas kernels for 0%

commit v1 on v0

--- a/solution.py
+++ b/solution.py
@@ -10,6 +10,19 @@
 epsilon = 1e-08
 correct_one = 0.9999734386011124
 correct_two = 0.09520785288629094
+
+
+def direct_the_rings(here_x):
+    carry_out = jnp.concatenate(
+        jax.lax.all_to_all(
+            jnp.stack([here_x for _ in range(jax.lax.axis_size("shard"))], axis=0),
+            axis_name="shard",
+            split_axis=0,
+            concat_axis=0,
+        ),
+        axis=1,
+    )
+    return carry_out
 
 
 def adamw_update(weight, moment, second, gradient, clip_factor):
@@ -64,7 +77,7 @@
     wc, mc, vc = adamw_update(weight_chan, moment_chan, second_chan, mean_c, clip_factor)
     we, me, ve = adamw_update(weight_embed, moment_embed, second_embed, mean_e, clip_factor)
     gathered = (
-        lax.all_gather(wx.astype(jnp.bfloat16), "shard", axis=1, tiled=True),
+        direct_the_rings(wx.astype(jnp.bfloat16)),
         lax.all_gather(wc.astype(jnp.bfloat16), "shard", axis=2, tiled=True),
         lax.all_gather(we.astype(jnp.bfloat16), "shard", axis=0, tiled=True),
     )

time: 810 us -> 789 us (0.974)
  waiting for transfers between devices: 126 us -> 74.5 us
  blocking collectives: 378 us -> 408 us
    all_gather x1 -> x0, waiting for transfers between devices: 32.9 us -> none  [on_device(): lax.all_gather(wx.astype(jnp.bfloat16), 'shard', axis=1, tiled=True)]
    all_to_all x0 -> x1, blocking collectives: none -> 29.8 us  [direct_the_rings(): jax.lax.all_to_all(jnp.stack([here_x for _ in range(jax.lax.axis_size('sh...]
    all_gather x1, waiting for transfers between devices: 16.8 us -> 0.01 us  [on_device(): lax.all_gather(wc.astype(jnp.bfloat16), 'shard', axis=2, tiled=True)]
    unnamed x13 -> x12, local copies, waits for them, and re-layouts: 241 us -> 241 us
    unnamed x7 -> x6, waiting for transfers between devices: 23 us -> 23 us
  transfers between devices with their start and end apart: 6 -> 5, of which waited for: 5 -> 3; matrix products, arithmetic and copies ran while one was open for 13% -> 13% of each run, Pallas kernels for 0% -> 0%
where the time goes in v1:
time: 789 us; the launch traced here: 786 us
  blocking collectives  408 us (52%)
  local copies, waits for them, and re-layouts  243 us (31%)
  waiting for transfers between devices  74.5 us (9%)
  other arithmetic  42.5 us (5%)
  between operations  17.6 us (2%)
    psum x1, blocking collectives, on_device(): blocks = lax.psum((group[0], group[1], group[2]), 'rep')  374 us
    unnamed x12, local copies, waits for them, and re-layouts  241 us
    all_gather x1, waiting for transfers between devices, on_device(): lax.all_gather(we.astype(jnp.bfloat16), 'shard', axis=0, tiled=True)  48.9 us
    all_to_all x1, blocking collectives, direct_the_rings(): jax.lax.all_to_all(jnp.stack([here_x for _ in range(jax.lax.axis_size('sh...  29.8 us
    unnamed x6, waiting for transfers between devices  23 us
  transfers between devices with their start and end apart: 5, of which 3 were waited for; matrix products, arithmetic and copies ran while one was open for 13% of the time, Pallas kernels for 0%

profile of v1, /device:TPU:1, one launch (start us, length us, event | category | flops | bytes accessed | tf_op | source)
XLA Modules:
  0.0 785.5 jit_solution(2517195768088750267)
XLA Ops:
  7.2 0.0 reduce-scatter.10.cloned.1.call-start
  7.2 6.5 reduce_sum.65
  13.7 66.3 %copy.27 = bf16[2,118,3072]{0,1,2:T(8,128)(2,1)} copy(bf16[2,118,3072]{2,0,1:T(2,128)(2,1)S(1)} %reduce_sum.65) | data formatting | bytes 2899968
  80.0 86.8 %reshape.38 = bf16[3072,236]{1,0:T(8,128)(2,1)} reshape(bf16[3072,118,2]{2,1,0:T(8,128)(2,1)} %bitcast.1) | data formatting | bytes 2899968
  166.8 0.0 reduce-scatter.10.cloned.1.call-update
  166.8 0.0 reduce-scatter.6.cloned.1.call-start
  166.9 2.2 reduce_sum.63
  169.0 0.0 reduce-scatter.6.cloned.1.call-update
  169.1 0.0 reduce-scatter.8.cloned.1.call-start
  169.1 6.5 reduce_sum.67
  175.6 0.0 reduce-scatter.8.cloned.1.call-update
  175.6 0.2 all-gather.3.cloned.1.call-start
  175.9 22.9 %reduce-scatter.10.cloned.1.call-done = bf16[1536,236]{1,0:T(8,128)(2,1)} async-done(((bf16[3072,236]{1,0:T(8,128)(2,1)}), bf16[1536,236]{1,0:T(8,128)(2,1)}) %reduce-scatter.10.cloned.1.call-update) | async-done | bytes 725008
  198.8 37.8 %reshape.39 = bf16[1536,118,2]{2,1,0:T(8,128)(2,1)} reshape(bf16[1536,236]{1,0:T(8,128)(2,1)} %reduce-scatter.10.cloned.1.call-done) | data formatting | bytes 1449984
  236.6 41.9 %copy.28 = bf16[2,118,1536]{2,0,1:T(2,128)(2,1)} copy(bf16[2,118,1536]{0,1,2:T(8,128)(2,1)} %bitcast.8) | data formatting | bytes 1449984
  278.5 2.7 reduce-scatter.8.cloned.1.call-done
  281.2 373.8 %all-reduce.2 = (f32[2,1536,128]{2,1,0:T(8,128)}, f32[2,118,1536]{2,0,1:T(2,128)}, f32[512,1536]{1,0:T(8,128)S(1)}) all-reduce(bf16[2,1536,128]{2,1,0:T(8,128)(2,1)} %reduce-scatter.6.cloned.1.call-done, bf16[2,118,1536]{2,0,1:T(2,128)(2,1)} %copy.28, ...), channel_id=1, replica_groups=mesh['rep'=64,'shard'=2] {'rep'}, use_global_device_ids=true, to_apply=%region_2.0 | all-reduce | flops 1542144 | bytes 9252864 | tf_op jit(solution)/shard_map/psum | solution.py:67
  654.9 2.5 multiply_reduce_fusion.1
  657.5 2.1 multiply_reduce_fusion.2
  659.6 1.4 multiply_reduce_fusion
  662.9 4.3 psum.31
  667.9 8.5 %fusion.5 = (bf16[2,118,1536]{2,0,1:T(2,128)(2,1)}, f32[2,118,1536]{2,0,1:T(2,128)}, f32[2,118,1536]{2,0,1:T(2,128)}, f32[2,118,1536]{2,0,1:T(2,128)}) fusion(f32[2,118,1536]{2,0,1:T(2,128)} %param.16, f32[2,118,1536]{2,0,1:T(2,128)} %get-tuple-element.14, f32[]{:T(128)S(6)} %mul.157, f32[2,118,1536]{2,0,1:T(2,128)} %param.19, f32[2,118,1536]{2,0,1:T(2,128)} %param.22), kind=kLoop, calls=%fused_computation.18 | loop fusion | flops 6162432 | bytes 10874884 | tf_op jit(solution)/shard_map/convert_element_type | solution.py:81
  676.4 0.0 all-gather.5.cloned.1.call-start
  676.5 7.3 fusion.3
  683.8 1.4 copy-done
  685.2 5.4 convert_bitcast_fusion
  690.6 0.1 pad_maximum_fusion
  690.7 29.8 %all_to_all.5 = bf16[2,2,1536,128]{3,2,1,0:T(8,128)(2,1)S(1)} all-to-all(bf16[2,2,1536,128]{3,2,1,0:T(8,128)(2,1)S(1)} %pad_maximum_fusion), channel_id=1, replica_groups=mesh['rep'=64,'shard'=2] {'shard'}, dimensions={0} | all-to-all | bytes 3145728 | tf_op jit(solution)/shard_map/all_to_all | solution.py:17
  720.5 1.2 copy.26
  721.8 48.9 %all-gather.5.cloned.1.call-done = bf16[1024,1536]{1,0:T(8,128)(2,1)} async-done(((bf16[512,1536]{1,0:T(8,128)(2,1)}), bf16[1024,1536]{1,0:T(8,128)(2,1)}) %all-gather.5.cloned.1.call-update) | async-done | bytes 3145744 | tf_op jit(solution)/shard_map/all_gather | solution.py:82
  770.6 3.5 copy.37
  774.1 3.8 copy.38
  (9 shorter events, 0.0 us)
Async XLA Ops:
  7.2 191.6 %reduce-scatter.10.cloned.1.call-start = ((), (), s32[]{:S(2)}) async-start(), calls=%async_computation.8 | async-start | bytes 2359296
  80.0 86.8 %copy-start.2 = (bf16[2,2,3072,128]{3,2,1,0:T(8,128)(2,1)S(1)}, bf16[2,2,3072,128]{3,2,1,0:T(8,128)(2,1)}, u32[]{:S(2)}) copy-start(bf16[2,2,3072,128]{3,2,1,0:T(8,128)(2,1)} %param.12) | copy-start | bytes 9437188
  166.8 111.7 %reduce-scatter.6.cloned.1.call-start = ((), (), s32[]{:S(2)}) async-start(), calls=%async_computation.4 | async-start | bytes 2359296 | tf_op jit(solution)/shard_map/reduce_scatter | solution.py:57
  169.1 112.1 %reduce-scatter.8.cloned.1.call-start = ((), (), s32[]{:S(2)}) async-start(), calls=%async_computation.5 | async-start | bytes 4718592 | tf_op jit(solution)/shard_map/reduce_scatter | solution.py:63
  175.6 546.1 %all-gather.3.cloned.1.call-start = ((), (), s32[]{:S(2)}) async-start(), calls=%async_computation.6 | async-start | bytes 2174976 | tf_op jit(solution)/shard_map/all_gather | solution.py:81
  654.9 2.5 copy-start.1
  676.4 94.2 %all-gather.5.cloned.1.call-start = ((), (), s32[]{:S(2)}) async-start(), calls=%async_computation.7 | async-start | bytes 4718592 | tf_op jit(solution)/shard_map/all_gather | solution.py:82
  683.8 1.4 copy-start
Sparse Core Ops, SparseCore 0:
  166.9 31.7 reduce-scatter.9
  201.8 29.5 reduce-scatter.5
  234.3 46.8 reduce-scatter.7
  676.5 37.8 all-gather.2
  716.6 54.0 all-gather.4
